TPU v7x, 256 devices: a whole 4x4x8 slice. The times are simulated.
256 devices in a mesh: grp: 16 (over y, x_lo, core), tm: 16 (over z, x_hi).
Axes of the slice: x: 4 (x_hi: 2, x_lo: 2; x = x_hi * 2 + x_lo), y: 4, z: 8, core: 2. Of those that a mesh axis runs over, the one named last changes fastest.
Arguments:
- motion: bfloat16 [1024, 128, 1024], P(('grp', 'tm')), may hold values from -30 to 30
- modulation: float32 [6, 1024], replicated, may hold values from -1.25 to 1.25
- w_temporal_qkv: bfloat16 [1024, 3072], replicated, may hold values from -1 to 1
- w_temporal_out: bfloat16 [1024, 1024], replicated, may hold values from -0.1875 to 0.1875
- w_inter_qkv: bfloat16 [1024, 3072], P('tm'), may hold values from -1 to 1
- w_inter_out: bfloat16 [1024, 1024], P('tm'), may hold values from -0.1875 to 0.1875
- links: int32 [16, 4], replicated, may hold values from 0 to 1, as said below
Outputs:
- motion_out: bfloat16 [1024, 128, 1024], P(('grp', 'tm'))
Inputs may be any that keep to these rules, and one draw needn't show every extreme that they name: Every group has between 1 and 4 links; one group has all of them and another exactly one.
All inputs are finite; a program needn't handle non-finite values.
Results may differ from a plain program's by a relative error of at most 0.008.
Values may be sent and summed in bfloat16 or wider, within the bound.
No kernel may reach another device: no remote copies, remote signals or barrier semaphores. Data moves between devices by JAX's collectives and lax.ppermute only.
A program may use at most 128 MiB of HBM per device.

v0:
```python
import jax
import jax.numpy as jnp
from jax import lax
from jax.sharding import PartitionSpec as P

HEAD = 64
REACH = 2
EPSILON = 1e-06


def from_behind(block, axis, distance):
    devices = range(lax.axis_size(axis))
    route = [((i - distance) % len(devices), i) for i in devices]
    return lax.ppermute(block, axis, route)


def modulate(field, modulation, first, second):
    values = field.astype(jnp.float32)
    mean_square = jnp.mean(values * values, axis=-1, keepdims=True)
    scaled = (
        values * lax.rsqrt(mean_square + EPSILON) * (1.0 + modulation[second]) + modulation[first]
    )
    return scaled.astype(jnp.bfloat16)


def softmax_rows(scores):
    row_top = jnp.max(scores, axis=-1, keepdims=True)
    weights = jnp.exp(scores - row_top)
    return (weights / jnp.sum(weights, axis=-1, keepdims=True)).astype(jnp.bfloat16)


def temporal_heads(char_items, qkv_weight):
    item_count, frame_count, feature_width = char_items.shape
    head_count = feature_width // HEAD
    packed = jnp.dot(
        char_items.reshape(item_count * frame_count, feature_width),
        qkv_weight,
        preferred_element_type=jnp.float32,
    )
    packed = packed.astype(jnp.bfloat16).reshape(item_count, frame_count, 3, head_count, HEAD)
    scores = jnp.einsum(
        "nfhd,nghd->nhfg", packed[:, :, 0], packed[:, :, 1], preferred_element_type=jnp.float32
    ) * HEAD ** (-0.5)
    weights = softmax_rows(scores)
    mixed_heads = jnp.einsum(
        "nhfg,nghd->nfhd", weights, packed[:, :, 2], preferred_element_type=jnp.float32
    )
    return mixed_heads.astype(jnp.bfloat16).reshape(item_count, frame_count, feature_width)


def per_device(motion, modulation, w_temporal_qkv, w_temporal_out, w_inter_qkv, w_inter_out, links):
    own_chars, all_frames, feature_width = motion.shape
    head_count = feature_width // HEAD
    inter_qkv, inter_out = (
        lax.all_gather(w_inter_qkv, "tm", axis=0, tiled=True),
        lax.all_gather(w_inter_out, "tm", axis=0, tiled=True),
    )
    normed = modulate(motion, modulation, 0, 1)
    t_mixed = temporal_heads(normed, w_temporal_qkv)
    t_projected = jnp.dot(
        t_mixed.reshape(own_chars * all_frames, feature_width),
        w_temporal_out,
        preferred_element_type=jnp.float32,
    )
    middle = (
        motion.astype(jnp.float32)
        + modulation[2] * t_projected.reshape(own_chars, all_frames, feature_width)
    ).astype(jnp.bfloat16)
    middle_frames = lax.all_to_all(middle, "tm", split_axis=1, concat_axis=0, tiled=True)
    char_count, frame_count, unused_width = middle_frames.shape
    token_count = char_count * frame_count
    normed_inter = modulate(middle_frames, modulation, 3, 4)
    packed = jnp.dot(
        normed_inter.reshape(token_count, feature_width),
        inter_qkv,
        preferred_element_type=jnp.float32,
    )
    packed = packed.astype(jnp.bfloat16).reshape(char_count, frame_count, 3 * feature_width)
    own_pairs = packed[:, :, feature_width:]
    neighbours = []
    current = own_pairs
    for step in range(REACH):
        current = from_behind(current, "grp", -1)
        neighbours.append(current)
    current = own_pairs
    for step in range(REACH):
        current = from_behind(current, "grp", 1)
        neighbours.append(current)
    stacked = jnp.concatenate([own_pairs] + neighbours, axis=0)
    queries = packed[:, :, :feature_width].reshape(char_count, frame_count, head_count, HEAD)
    key_part = stacked[:, :, :feature_width].reshape(-1, frame_count, head_count, HEAD)
    value_part = stacked[:, :, feature_width:].reshape(-1, frame_count, head_count, HEAD)
    scores = jnp.einsum(
        "cfhd,kfhd->fhck", queries, key_part, preferred_element_type=jnp.float32
    ) * HEAD ** (-0.5)
    group_ids = jnp.arange(links.shape[0], dtype=jnp.int32)
    own_links = jnp.sum(jnp.where(group_ids[:, None] == lax.axis_index("grp"), links, 0), axis=0)
    allowed = jnp.concatenate([jnp.ones((1,), jnp.int32), own_links])
    key_mask = jnp.repeat(allowed, char_count) > 0
    scores = jnp.where(key_mask, scores, -jnp.inf)
    weights = softmax_rows(scores)
    mixed_heads = jnp.einsum(
        "fhck,kfhd->cfhd", weights, value_part, preferred_element_type=jnp.float32
    ).astype(jnp.bfloat16)
    mixed_chars = lax.all_to_all(
        mixed_heads.reshape(char_count, frame_count, feature_width),
        "tm",
        split_axis=0,
        concat_axis=1,
        tiled=True,
    )
    result = jnp.dot(
        mixed_chars.reshape(own_chars * all_frames, feature_width),
        inter_out,
        preferred_element_type=jnp.float32,
    )
    total = middle.astype(jnp.float32) + modulation[5] * result.reshape(
        own_chars, all_frames, feature_width
    )
    return total.astype(jnp.bfloat16)


def solution(mesh):
    placed = (P(("grp", "tm"), None, None), P(), P(), P(), P("tm", None), P("tm", None), P())
    return jax.shard_map(
        per_device,
        mesh=mesh,
        in_specs=placed,
        out_specs=P(("grp", "tm"), None, None),
        check_vma=False,
    )
```

profile of v0, /device:TPU:16, one launch (start us, length us, event | category | flops | bytes accessed | tf_op | source)
XLA Modules:
  0.0 351.3 jit_solution(12227734614028227783)
XLA Ops:
  9.8 1.6 fusion.17
  11.4 7.6 %convolution_convert_fusion.1 = bf16[512,3072]{1,0:T(8,128)(2,1)} fusion(bf16[512,1024]{1,0:T(8,128)(2,1)S(1)} %bitcast.66, bf16[1024,3072]{1,0:T(8,128)(2,1)} %param.9), kind=kOutput, calls=%fused_computation.11 | convolution fusion | flops 3222798336 | bytes 10485760 | tf_op jit(solution)/shard_map/dot_general | solution.py:35
  19.0 8.6 %reshape.111 = bf16[4,128,3,16,64]{4,3,2,1,0:T(8,128)(2,1)} reshape(bf16[512,3072]{1,0:T(8,128)(2,1)} %convolution_convert_fusion.1) | data formatting | bytes 6291456 | tf_op jit(solution)/shard_map/reshape | solution.py:40
  27.6 6.1 %fusion.51 = (bf16[4,128,1,16,64]{4,3,2,1,0:T(8,128)(2,1)}, bf16[4,128,1,16,64]{4,3,2,1,0:T(8,128)(2,1)}, bf16[4,128,1,16,64]{4,3,2,1,0:T(8,128)(2,1)}) fusion(bf16[4,128,3,16,64]{4,3,2,1,0:T(8,128)(2,1)} %reshape.111), kind=kLoop, calls=%fused_computation.67 | loop fusion | bytes 6291456 | tf_op jit(solution)/shard_map/slice | solution.py:46
  33.7 2.8 copy.62
  36.5 3.5 %copy.63 = bf16[4,128,1,16,64]{1,4,3,0,2:T(8,128)(2,1)} copy(bf16[4,128,1,16,64]{4,3,2,1,0:T(8,128)(2,1)} %get-tuple-element.9) | data formatting | bytes 2097152
  40.1 3.6 %copy.61 = bf16[4,128,1,16,64]{1,4,3,0,2:T(8,128)(2,1)} copy(bf16[4,128,1,16,64]{4,3,2,1,0:T(8,128)(2,1)} %get-tuple-element.7) | data formatting | bytes 2097152
  43.6 2.0 fusion.42
  45.6 4.0 %fusion.54 = (f32[4,16,128]{2,1,0:T(8,128)S(1)}, f32[4,16,128,128]{2,3,1,0:T(8,128)S(1)}) fusion(f32[4,16,128,128]{2,3,1,0:T(8,128)S(1)} %fusion.42), kind=kOutput, calls=%fused_computation.70 | output fusion | flops 4194431 | bytes 8421376 | tf_op jit(solution)/shard_map/sub | solution.py:28
  53.0 48.2 %all_to_all.24 = bf16[4,128,1024]{2,0,1:T(4,128)(2,1)S(1)} all-to-all(bf16[4,128,1024]{2,0,1:T(4,128)(2,1)S(1)} %copy.48), channel_id=1, replica_groups=mesh['grp'=16,'tm'=16] {'tm'}, dimensions={1} | all-to-all | bytes 2097152 | tf_op jit(solution)/shard_map/all_to_all | solution.py:69
  103.7 1.9 fusion.23
  105.6 33.3 %all-gather.3.cloned.1.call-done = bf16[1024,3072]{1,0:T(8,128)(2,1)} async-done(((bf16[64,3072]{1,0:T(8,128)(2,1)}), bf16[1024,3072]{1,0:T(8,128)(2,1)}) %all-gather.3.cloned.1.call-update) | async-done | bytes 6291472 | tf_op jit(solution)/shard_map/all_gather | solution.py:55
  138.9 6.4 %fusion.7 = bf16[64,8,3072]{2,1,0:T(8,128)(2,1)S(1)} fusion(bf16[512,1024]{1,0:T(8,128)(2,1)S(1)} %fusion.23, bf16[1024,3072]{1,0:T(8,128)(2,1)} %all-gather.3.cloned.1.call-done), kind=kOutput, calls=%fused_computation.14 | convolution fusion | flops 3222798336 | bytes 10485760 | tf_op jit(solution)/shard_map/dot_general | solution.py:73
  145.3 1.7 copy-done.3
  147.0 1.9 fusion.52
  149.4 45.5 %collective-permute-done = bf16[64,8,2048]{2,1,0:T(8,128)(2,1)} collective-permute-done((bf16[64,8,2048]{2,1,0:T(8,128)(2,1)S(1)}, bf16[64,8,2048]{2,1,0:T(8,128)(2,1)}, u32[]{:S(2)}, u32[]{:S(2)}) %collective-permute-start) | collective-permute-done | bytes 2097184 | tf_op jit(solution)/shard_map/ppermute | solution.py:14
  194.9 2.9 collective-permute-start.1
  199.5 2.5 reshape.99
  202.1 3.1 constant_dynamic-update-slice_fusion.3
  205.2 39.5 %collective-permute-done.1 = bf16[64,8,2048]{2,1,0:T(8,128)(2,1)} collective-permute-done((bf16[64,8,2048]{2,1,0:T(8,128)(2,1)}, bf16[64,8,2048]{2,1,0:T(8,128)(2,1)}, u32[]{:S(2)}, u32[]{:S(2)}) %collective-permute-start.1) | collective-permute-done | bytes 2097184 | tf_op jit(solution)/shard_map/ppermute | solution.py:14
  244.7 3.2 constant_dynamic-update-slice_fusion.2
  247.9 3.2 constant_dynamic-update-slice_fusion.1
  251.0 3.2 constant_dynamic-update-slice_fusion
  254.2 9.3 %fusion.50 = (bf16[320,8,1024]{2,1,0:T(8,128)(2,1)}, bf16[320,8,1024]{2,1,0:T(8,128)(2,1)}) fusion(bf16[320,8,2048]{2,1,0:T(8,128)(2,1)} %constant_dynamic-update-slice_fusion), kind=kLoop, calls=%fused_computation.66 | loop fusion | bytes 20971520 | tf_op jit(solution)/shard_map/slice | solution.py:91
  263.6 8.7 %copy.53 = bf16[320,8,1024]{0,2,1:T(8,128)(2,1)} copy(bf16[320,8,1024]{2,1,0:T(8,128)(2,1)} %get-tuple-element.5) | data formatting | bytes 10485760 | tf_op jit(solution)/shard_map/slice | solution.py:91
  272.2 12.4 %fusion.55 = (f32[8,16,64]{2,1,0:T(8,128)S(1)}, f32[8,16,64,320]{3,2,1,0:T(8,128)}) fusion(pred[320]{0:T(512)(128)(4,1)S(1)} %gt.12, bf16[320,8,16,64]{0,3,2,1:T(8,128)(2,1)} %bitcast.63, bf16[64,8,16,64]{3,2,1,0:T(8,128)(2,1)S(1)} %copy-done.4), kind=kOutput, calls=%fused_computation.71 | convolution fusion | flops 346030400 | bytes 16810304 | tf_op jit(solution)/shard_map/sub | solution.py:28
  284.6 8.5 %copy.52 = bf16[320,8,1024]{0,2,1:T(8,128)(2,1)} copy(bf16[320,8,1024]{2,1,0:T(8,128)(2,1)} %get-tuple-element.6) | data formatting | bytes 10485760 | tf_op jit(solution)/shard_map/slice | solution.py:92
  293.1 8.8 %fusion.28 = bf16[8,16,64,64]{3,2,1,0:T(8,128)(2,1)S(1)} fusion(bf16[320,8,16,64]{0,3,2,1:T(8,128)(2,1)} %bitcast.64, f32[8,16,64,320]{3,2,1,0:T(8,128)} %get-tuple-element.21, f32[8,16,64]{2,1,0:T(8,128)S(1)} %get-tuple-element.20), kind=kOutput, calls=%fused_computation.40 | convolution fusion | flops 341311488 | bytes 16809984 | tf_op jit(solution)/shard_map/fhck,kfhd->cfhd/dot_general | solution.py:102
  301.9 2.4 copy.55
  304.3 4.9 %all-to-all-start.1 = ((bf16[64,8,1024]{2,1,0:T(8,128)(2,1)}), bf16[64,8,1024]{2,1,0:T(8,128)(2,1)}, u32[]{:S(2)}, u32[]{:S(2)}) async-start(bf16[64,8,1024]{2,1,0:T(8,128)(2,1)} %copy.55), calls=%async_computation.1 | async-start | bytes 2097152 | tf_op jit(solution)/shard_map/all_to_all | solution.py:105
  309.3 31.0 %all-to-all-done.1 = bf16[64,8,1024]{2,1,0:T(8,128)(2,1)} async-done(((bf16[64,8,1024]{2,1,0:T(8,128)(2,1)}), bf16[64,8,1024]{2,1,0:T(8,128)(2,1)}, u32[]{:S(2)}, u32[]{:S(2)}) %all-to-all-start.1) | async-done | bytes 1048608 | tf_op jit(solution)/shard_map/all_to_all | solution.py:105
  340.3 4.1 %add_convert_fusion = bf16[4,128,1024]{2,1,0:T(8,128)(2,1)} fusion(bf16[4,128,1024]{2,1,0:T(8,128)(2,1)S(1)} %fusion.18, bf16[1024,1024]{1,0:T(8,128)(2,1)} %all-gather.5.cloned.1.call-done, bf16[4,16,8,1024]{3,2,0,1:T(8,128)(2,1)} %bitcast.23, f32[1024]{0:T(1024)S(1)} %bitcast.72), kind=kOutput, calls=%fused_computation.37 | convolution fusion | flops 1075838976 | bytes 5246976 | tf_op jit(solution)/shard_map/dot_general | solution.py:112
  (42 shorter events, 11.3 us)
Async XLA Ops:
  6.5 43.8 %copy-start = (bf16[1024,1024]{1,0:T(8,128)(2,1)S(1)}, bf16[1024,1024]{1,0:T(8,128)(2,1)}, u32[]{:S(2)}) copy-start(bf16[1024,1024]{1,0:T(8,128)(2,1)} %param.10) | copy-start | bytes 6291460
  6.5 132.4 %all-gather.3.cloned.1.call-start = ((), (), s32[]{:S(2)}) async-start(), calls=%async_computation.2 | async-start | bytes 6684672 | tf_op jit(solution)/shard_map/all_gather | solution.py:55
  7.3 302.0 %all-gather.5.cloned.1.call-start = ((), (), s32[]{:S(2)}) async-start(), calls=%async_computation.3 | async-start | bytes 2228224 | tf_op jit(solution)/shard_map/all_gather | solution.py:56
  45.6 4.0 %copy-start.5 = (bf16[4,128,1,16,64]{1,4,3,0,2:T(8,128)(2,1)S(1)}, bf16[4,128,1,16,64]{1,4,3,0,2:T(8,128)(2,1)}, u32[]{:S(2)}) copy-start(bf16[4,128,1,16,64]{1,4,3,0,2:T(8,128)(2,1)} %copy.61) | copy-start | bytes 3145732
  49.7 1.2 copy-start.2
  145.3 1.7 copy-start.3
  147.0 50.8 %copy-start.6 = (s32[16,4]{0,1:T(4,128)S(1)}, s32[16,4]{0,1:T(4,128)}, u32[]{:S(2)}) copy-start(s32[16,4]{0,1:T(4,128)} %param.13) | copy-start | bytes 772
  148.9 46.0 %collective-permute-start = (bf16[64,8,2048]{2,1,0:T(8,128)(2,1)S(1)}, bf16[64,8,2048]{2,1,0:T(8,128)(2,1)}, u32[]{:S(2)}, u32[]{:S(2)}) collective-permute-start(bf16[64,8,2048]{2,1,0:T(8,128)(2,1)S(1)} %get-tuple-element.10), channel_id=1, source_target_pairs={{16,0},{32,16},{48,32},{64,48},{80,64},{96,80},{112,96},{128,112},... | collective-permute-start | bytes 6291464 | tf_op jit(solution)/shard_map/ppermute | solution.py:14
  148.9 48.9 %collective-permute-start.2 = (bf16[64,8,2048]{2,1,0:T(8,128)(2,1)S(1)}, bf16[64,8,2048]{2,1,0:T(8,128)(2,1)}, u32[]{:S(2)}, u32[]{:S(2)}) collective-permute-start(bf16[64,8,2048]{2,1,0:T(8,128)(2,1)S(1)} %get-tuple-element.10), channel_id=1, source_target_pairs={{240,0},{0,16},{16,32},{32,48},{48,64},{64,80},{80,96},{96,112},{1... | collective-permute-start | bytes 6291464 | tf_op jit(solution)/shard_map/ppermute | solution.py:14
  194.9 49.8 %collective-permute-start.1 = (bf16[64,8,2048]{2,1,0:T(8,128)(2,1)}, bf16[64,8,2048]{2,1,0:T(8,128)(2,1)}, u32[]{:S(2)}, u32[]{:S(2)}) collective-permute-start(bf16[64,8,2048]{2,1,0:T(8,128)(2,1)} %collective-permute-done), channel_id=1, source_target_pairs={{16,0},{32,16},{48,32},{64,48},{80,64},{96,80},{112,96},{128,112},... | collective-permute-start | bytes 6291464 | tf_op jit(solution)/shard_map/ppermute | solution.py:14
  197.8 53.2 %collective-permute-start.3 = (bf16[64,8,2048]{2,1,0:T(8,128)(2,1)}, bf16[64,8,2048]{2,1,0:T(8,128)(2,1)}, u32[]{:S(2)}, u32[]{:S(2)}) collective-permute-start(bf16[64,8,2048]{2,1,0:T(8,128)(2,1)} %collective-permute-done.2), channel_id=1, source_target_pairs={{240,0},{0,16},{16,32},{32,48},{48,64},{64,80},{80,96},{96,112},{1... | collective-permute-start | bytes 6291464 | tf_op jit(solution)/shard_map/ppermute | solution.py:14
  263.6 8.7 %copy-start.4 = (bf16[64,8,16,64]{3,2,1,0:T(8,128)(2,1)S(1)}, bf16[64,8,16,64]{3,2,1,0:T(8,128)(2,1)}, u32[]{:S(2)}) copy-start(bf16[64,8,16,64]{3,2,1,0:T(8,128)(2,1)} %reshape.99) | copy-start | bytes 3145732
  304.3 36.0 %all-to-all-start.1 = ((bf16[64,8,1024]{2,1,0:T(8,128)(2,1)}), bf16[64,8,1024]{2,1,0:T(8,128)(2,1)}, u32[]{:S(2)}, u32[]{:S(2)}) async-start(bf16[64,8,1024]{2,1,0:T(8,128)(2,1)} %copy.55), calls=%async_computation.1 | async-start | bytes 2097152 | tf_op jit(solution)/shard_map/all_to_all | solution.py:105
  309.2 35.2 %copy-start.1 = (bf16[1024,1024]{1,0:T(8,128)(2,1)S(1)}, bf16[1024,1024]{1,0:T(8,128)(2,1)}, u32[]{:S(2)}) copy-start(bf16[1024,1024]{1,0:T(8,128)(2,1)} %param.10) | copy-start | bytes 6291460
Sparse Core Ops, SparseCore 0:
  9.9 128.9 all-gather.2
  198.0 83.9 all-gather.4
where the time goes:
time: 353 us; the launch traced here: 351 us
  waiting for transfers between devices  150 us (42%)
  local copies, waits for them, and re-layouts  76.8 us (22%)
  blocking collectives  48.2 us (14%)
  matrix products  43.2 us (12%)
  between operations  13.6 us (4%)
  other arithmetic  11 us (3%)
  starting transfers between devices  8.41 us (2%)
    ppermute x4, waiting for transfers between devices, from_behind(): return lax.ppermute(block, axis, route)  85 us
    all_to_all x1, blocking collectives, per_device(): lax.all_to_all(middle, 'tm', split_axis=1, concat_axis=0, tiled=True)  48.2 us
    all_gather x1, waiting for transfers between devices, per_device(): lax.all_gather(w_inter_qkv, 'tm', axis=0, tiled=True)  33.3 us
    all_to_all x1, waiting for transfers between devices, per_device(): lax.all_to_all(mixed_heads.reshape(char_count, frame_count, feature_width...  31 us
    unnamed x20, local copies, waits for them, and re-layouts  21.7 us
    slice x2, local copies, waits for them, and re-layouts, per_device(): stacked[:, :, :feature_width].reshape(-1, frame_count, head_count, HEAD)  18 us
    sub x1, matrix products, softmax_rows(): weights = jnp.exp(scores - row_top)  12.4 us
    dot_general x1, matrix products, per_device(): jnp.einsum('fhck,kfhd->cfhd', weights, value_part, preferred_element_type...  8.79 us
  transfers between devices with their start and end apart: 7, of which 4 were waited for; matrix products, arithmetic and copies ran while one was open for 33% of the time, Pallas kernels for 0%

commit v1 on v0

--- a/solution.py
+++ b/solution.py
@@ -51,8 +51,14 @@
 def per_device(motion, modulation, w_temporal_qkv, w_temporal_out, w_inter_qkv, w_inter_out, links):
     own_chars, all_frames, feature_width = motion.shape
     head_count = feature_width // HEAD
+
+    def _detail_weights(u):
+        carry_in = tuple((u for _ in range(lax.axis_size("tm"))))
+        f_now = jnp.stack(carry_in, axis=0)
+        return jnp.concatenate(lax.all_to_all(f_now, "tm", split_axis=0, concat_axis=0), axis=0)
+
     inter_qkv, inter_out = (
-        lax.all_gather(w_inter_qkv, "tm", axis=0, tiled=True),
+        _detail_weights(w_inter_qkv),
         lax.all_gather(w_inter_out, "tm", axis=0, tiled=True),
     )
     normed = modulate(motion, modulation, 0, 1)

time: 353 us -> 458 us (1.30)
  waiting for transfers between devices: 150 us -> 258 us
  blocking collectives: 48.2 us -> 40.9 us
  starting transfers between devices: 8.41 us -> 13.4 us
    all_to_all x0 -> x1, waiting for transfers between devices: none -> 143 us  [_detail_weights(): lax.all_to_all(f_now, 'tm', split_axis=0, concat_axis=0)]
    all_gather x1 -> x0, waiting for transfers between devices: 33.3 us -> none  [per_device(): lax.all_gather(w_inter_qkv, 'tm', axis=0, tiled=True)]
    all_to_all x1, blocking collectives: 48.2 us -> 40.9 us  [per_device(): lax.all_to_all(middle, 'tm', split_axis=1, concat_axis=0, tiled=True)]
    all_to_all x0 -> x1, starting transfers between devices: none -> 4.64 us  [_detail_weights(): lax.all_to_all(f_now, 'tm', split_axis=0, concat_axis=0)]
  transfers between devices with their start and end apart: 7 -> 7, of which waited for: 4 -> 4; matrix products, arithmetic and copies ran while one was open for 33% -> 15% of each run, Pallas kernels for 0% -> 0%
where the time goes in v1:
time: 458 us; the launch traced here: 457 us
  waiting for transfers between devices  258 us (56%)
  local copies, waits for them, and re-layouts  77.2 us (17%)
  matrix products  45.6 us (10%)
  blocking collectives  40.9 us (9%)
  between operations  13.6 us (3%)
  starting transfers between devices  13.4 us (3%)
  other arithmetic  8.38 us (2%)
    all_to_all x1, waiting for transfers between devices, _detail_weights(): lax.all_to_all(f_now, 'tm', split_axis=0, concat_axis=0)  143 us
    ppermute x4, waiting for transfers between devices, from_behind(): return lax.ppermute(block, axis, route)  85.2 us
    all_to_all x1, blocking collectives, per_device(): lax.all_to_all(middle, 'tm', split_axis=1, concat_axis=0, tiled=True)  40.9 us
    all_to_all x1, waiting for transfers between devices, per_device(): lax.all_to_all(mixed_heads.reshape(char_count, frame_count, feature_width...  29.3 us
    unnamed x20, local copies, waits for them, and re-layouts  20.5 us
    slice x2, local copies, waits for them, and re-layouts, per_device(): stacked[:, :, :feature_width].reshape(-1, frame_count, head_count, HEAD)  18.1 us
    sub x1, matrix products, softmax_rows(): weights = jnp.exp(scores - row_top)  12.4 us
  transfers between devices with their start and end apart: 7, of which 4 were waited for; matrix products, arithmetic and copies ran while one was open for 15% of the time, Pallas kernels for 0%

profile of v1, /device:TPU:16, one launch (start us, length us, event | category | flops | bytes accessed | tf_op | source)
XLA Modules:
  0.0 456.6 jit_solution(15010892530229111933)
XLA Ops:
  10.7 7.6 %convolution_convert_fusion.1 = bf16[512,3072]{1,0:T(8,128)(2,1)} fusion(bf16[512,1024]{1,0:T(8,128)(2,1)S(1)} %bitcast.73, bf16[1024,3072]{1,0:T(8,128)(2,1)} %param.9), kind=kOutput, calls=%fused_computation.11 | convolution fusion | flops 3222798336 | bytes 10485760 | tf_op jit(solution)/shard_map/dot_general | solution.py:35
  18.3 8.6 %reshape.116 = bf16[4,128,3,16,64]{4,3,2,1,0:T(8,128)(2,1)} reshape(bf16[512,3072]{1,0:T(8,128)(2,1)} %convolution_convert_fusion.1) | data formatting | bytes 6291456 | tf_op jit(solution)/shard_map/reshape | solution.py:40
  26.9 6.0 %fusion.53 = (bf16[4,128,1,16,64]{4,3,2,1,0:T(8,128)(2,1)}, bf16[4,128,1,16,64]{4,3,2,1,0:T(8,128)(2,1)}, bf16[4,128,1,16,64]{4,3,2,1,0:T(8,128)(2,1)}) fusion(bf16[4,128,3,16,64]{4,3,2,1,0:T(8,128)(2,1)} %reshape.116), kind=kLoop, calls=%fused_computation.67 | loop fusion | bytes 6291456 | tf_op jit(solution)/shard_map/slice | solution.py:46
  32.9 2.8 copy.59
  35.7 3.5 copy.60
  39.3 2.0 fusion.44
  41.3 2.9 fusion.56
  44.2 2.8 copy.58
  47.1 3.0 fusion.42
  52.2 40.9 %all_to_all.29 = bf16[4,128,1024]{2,0,1:T(4,128)(2,1)S(1)} all-to-all(bf16[4,128,1024]{2,0,1:T(4,128)(2,1)S(1)} %copy.46), channel_id=1, replica_groups=mesh['grp'=16,'tm'=16] {'tm'}, dimensions={1} | all-to-all | bytes 2097152 | tf_op jit(solution)/shard_map/all_to_all | solution.py:75
  93.0 3.4 stack.2
  96.5 4.6 %all-to-all-start.1 = ((bf16[16,64,3072]{2,1,0:T(8,128)(2,1)}), bf16[16,64,3072]{2,1,0:T(8,128)(2,1)}, u32[]{:S(2)}, u32[]{:S(2)}) async-start(bf16[16,64,3072]{2,1,0:T(8,128)(2,1)} %stack.2), calls=%async_computation.1 | async-start | bytes 12582912 | tf_op jit(solution)/shard_map/all_to_all | solution.py:58
  102.6 143.0 %all-to-all-done.1 = bf16[16,64,3072]{2,1,0:T(8,128)(2,1)} async-done(((bf16[16,64,3072]{2,1,0:T(8,128)(2,1)}), bf16[16,64,3072]{2,1,0:T(8,128)(2,1)}, u32[]{:S(2)}, u32[]{:S(2)}) %all-to-all-start.1) | async-done | bytes 6291488 | tf_op jit(solution)/shard_map/all_to_all | solution.py:58
  245.6 6.4 %fusion.7 = bf16[64,8,3072]{2,1,0:T(8,128)(2,1)S(1)} fusion(bf16[512,1024]{1,0:T(8,128)(2,1)S(1)} %bitcast.74, bf16[1024,3072]{1,0:T(8,128)(2,1)} %bitcast.17), kind=kOutput, calls=%fused_computation.14 | convolution fusion | flops 3222798336 | bytes 10485760 | tf_op jit(solution)/shard_map/dot_general | solution.py:79
  253.7 1.9 fusion.54
  256.1 45.4 %collective-permute-done = bf16[64,8,2048]{2,1,0:T(8,128)(2,1)} collective-permute-done((bf16[64,8,2048]{2,1,0:T(8,128)(2,1)S(1)}, bf16[64,8,2048]{2,1,0:T(8,128)(2,1)}, u32[]{:S(2)}, u32[]{:S(2)}) %collective-permute-start) | collective-permute-done | bytes 2097184 | tf_op jit(solution)/shard_map/ppermute | solution.py:14
  301.5 2.9 collective-permute-start.1
  306.1 2.3 reshape.110
  308.5 3.1 constant_dynamic-update-slice_fusion.3
  311.6 39.8 %collective-permute-done.1 = bf16[64,8,2048]{2,1,0:T(8,128)(2,1)} collective-permute-done((bf16[64,8,2048]{2,1,0:T(8,128)(2,1)}, bf16[64,8,2048]{2,1,0:T(8,128)(2,1)}, u32[]{:S(2)}, u32[]{:S(2)}) %collective-permute-start.1) | collective-permute-done | bytes 2097184 | tf_op jit(solution)/shard_map/ppermute | solution.py:14
  351.4 3.1 constant_dynamic-update-slice_fusion.2
  354.5 3.2 constant_dynamic-update-slice_fusion.1
  357.7 3.2 constant_dynamic-update-slice_fusion
  360.9 9.3 %fusion.52 = (bf16[320,8,1024]{2,1,0:T(8,128)(2,1)}, bf16[320,8,1024]{2,1,0:T(8,128)(2,1)}) fusion(bf16[320,8,2048]{2,1,0:T(8,128)(2,1)} %constant_dynamic-update-slice_fusion), kind=kLoop, calls=%fused_computation.66 | loop fusion | bytes 20971520 | tf_op jit(solution)/shard_map/slice | solution.py:97
  370.3 8.7 %copy.50 = bf16[320,8,1024]{0,2,1:T(8,128)(2,1)} copy(bf16[320,8,1024]{2,1,0:T(8,128)(2,1)} %get-tuple-element.5) | data formatting | bytes 10485760 | tf_op jit(solution)/shard_map/slice | solution.py:97
  379.0 12.4 %fusion.57 = (f32[8,16,64]{2,1,0:T(8,128)S(1)}, f32[8,16,64,320]{3,2,1,0:T(8,128)}) fusion(pred[320]{0:T(512)(128)(4,1)S(1)} %gt.12, bf16[320,8,16,64]{0,3,2,1:T(8,128)(2,1)} %bitcast.70, bf16[64,8,16,64]{3,2,1,0:T(8,128)(2,1)S(1)} %copy-done.4), kind=kOutput, calls=%fused_computation.71 | convolution fusion | flops 346030400 | bytes 16810304 | tf_op jit(solution)/shard_map/sub | solution.py:28
  391.4 8.5 %copy.49 = bf16[320,8,1024]{0,2,1:T(8,128)(2,1)} copy(bf16[320,8,1024]{2,1,0:T(8,128)(2,1)} %get-tuple-element.6) | data formatting | bytes 10485760 | tf_op jit(solution)/shard_map/slice | solution.py:98
  399.9 8.8 %fusion.30 = bf16[8,16,64,64]{3,2,1,0:T(8,128)(2,1)S(1)} fusion(bf16[320,8,16,64]{0,3,2,1:T(8,128)(2,1)} %bitcast.71, f32[8,16,64,320]{3,2,1,0:T(8,128)} %get-tuple-element.21, f32[8,16,64]{2,1,0:T(8,128)S(1)} %get-tuple-element.20), kind=kOutput, calls=%fused_computation.40 | convolution fusion | flops 341311488 | bytes 16809984 | tf_op jit(solution)/shard_map/fhck,kfhd->cfhd/dot_general | solution.py:108
  408.7 2.4 copy.52
  411.1 5.1 %all-to-all-start.2 = ((bf16[64,8,1024]{2,1,0:T(8,128)(2,1)}), bf16[64,8,1024]{2,1,0:T(8,128)(2,1)}, u32[]{:S(2)}, u32[]{:S(2)}) async-start(bf16[64,8,1024]{2,1,0:T(8,128)(2,1)} %copy.52), calls=%async_computation.2 | async-start | bytes 2097152 | tf_op jit(solution)/shard_map/all_to_all | solution.py:111
  416.2 29.3 %all-to-all-done.2 = bf16[64,8,1024]{2,1,0:T(8,128)(2,1)} async-done(((bf16[64,8,1024]{2,1,0:T(8,128)(2,1)}), bf16[64,8,1024]{2,1,0:T(8,128)(2,1)}, u32[]{:S(2)}, u32[]{:S(2)}) %all-to-all-start.2) | async-done | bytes 1048608 | tf_op jit(solution)/shard_map/all_to_all | solution.py:111
  445.6 4.1 add_convert_fusion
  (38 shorter events, 11.6 us)
Async XLA Ops:
  6.5 43.5 %copy-start = (bf16[1024,1024]{1,0:T(8,128)(2,1)S(1)}, bf16[1024,1024]{1,0:T(8,128)(2,1)}, u32[]{:S(2)}) copy-start(bf16[1024,1024]{1,0:T(8,128)(2,1)} %param.10) | copy-start | bytes 6291460
  47.0 3.0 copy-start.2
  50.0 43.0 %copy-start.5 = (bf16[64,3072]{1,0:T(8,128)(2,1)S(1)}, bf16[64,3072]{1,0:T(8,128)(2,1)}, u32[]{:S(2)}) copy-start(bf16[64,3072]{1,0:T(8,128)(2,1)} %param.11) | copy-start | bytes 1179652
  96.5 149.1 %all-to-all-start.1 = ((bf16[16,64,3072]{2,1,0:T(8,128)(2,1)}), bf16[16,64,3072]{2,1,0:T(8,128)(2,1)}, u32[]{:S(2)}, u32[]{:S(2)}) async-start(bf16[16,64,3072]{2,1,0:T(8,128)(2,1)} %stack.2), calls=%async_computation.1 | async-start | bytes 12582912 | tf_op jit(solution)/shard_map/all_to_all | solution.py:58
  101.1 315.1 %all-gather.2.cloned.1.call-start = ((), (), s32[]{:S(2)}) async-start(), calls=%async_computation.3 | async-start | bytes 2228224 | tf_op jit(solution)/shard_map/all_gather | solution.py:62
  252.0 1.8 copy-start.3
  253.7 50.8 %copy-start.6 = (s32[16,4]{0,1:T(4,128)S(1)}, s32[16,4]{0,1:T(4,128)}, u32[]{:S(2)}) copy-start(s32[16,4]{0,1:T(4,128)} %param.13) | copy-start | bytes 772
  255.6 45.9 %collective-permute-start = (bf16[64,8,2048]{2,1,0:T(8,128)(2,1)S(1)}, bf16[64,8,2048]{2,1,0:T(8,128)(2,1)}, u32[]{:S(2)}, u32[]{:S(2)}) collective-permute-start(bf16[64,8,2048]{2,1,0:T(8,128)(2,1)S(1)} %get-tuple-element.10), channel_id=1, source_target_pairs={{16,0},{32,16},{48,32},{64,48},{80,64},{96,80},{112,96},{128,112},... | collective-permute-start | bytes 6291464 | tf_op jit(solution)/shard_map/ppermute | solution.py:14
  255.6 48.8 %collective-permute-start.2 = (bf16[64,8,2048]{2,1,0:T(8,128)(2,1)S(1)}, bf16[64,8,2048]{2,1,0:T(8,128)(2,1)}, u32[]{:S(2)}, u32[]{:S(2)}) collective-permute-start(bf16[64,8,2048]{2,1,0:T(8,128)(2,1)S(1)} %get-tuple-element.10), channel_id=1, source_target_pairs={{240,0},{0,16},{16,32},{32,48},{48,64},{64,80},{80,96},{96,112},{1... | collective-permute-start | bytes 6291464 | tf_op jit(solution)/shard_map/ppermute | solution.py:14
  301.5 49.9 %collective-permute-start.1 = (bf16[64,8,2048]{2,1,0:T(8,128)(2,1)}, bf16[64,8,2048]{2,1,0:T(8,128)(2,1)}, u32[]{:S(2)}, u32[]{:S(2)}) collective-permute-start(bf16[64,8,2048]{2,1,0:T(8,128)(2,1)} %collective-permute-done), channel_id=1, source_target_pairs={{16,0},{32,16},{48,32},{64,48},{80,64},{96,80},{112,96},{128,112},... | collective-permute-start | bytes 6291464 | tf_op jit(solution)/shard_map/ppermute | solution.py:14
  304.4 53.3 %collective-permute-start.3 = (bf16[64,8,2048]{2,1,0:T(8,128)(2,1)}, bf16[64,8,2048]{2,1,0:T(8,128)(2,1)}, u32[]{:S(2)}, u32[]{:S(2)}) collective-permute-start(bf16[64,8,2048]{2,1,0:T(8,128)(2,1)} %collective-permute-done.2), channel_id=1, source_target_pairs={{240,0},{0,16},{16,32},{32,48},{48,64},{64,80},{80,96},{96,112},{1... | collective-permute-start | bytes 6291464 | tf_op jit(solution)/shard_map/ppermute | solution.py:14
  370.2 8.7 %copy-start.4 = (bf16[64,8,16,64]{3,2,1,0:T(8,128)(2,1)S(1)}, bf16[64,8,16,64]{3,2,1,0:T(8,128)(2,1)}, u32[]{:S(2)}) copy-start(bf16[64,8,16,64]{3,2,1,0:T(8,128)(2,1)} %reshape.110) | copy-start | bytes 3145732
  411.1 34.5 %all-to-all-start.2 = ((bf16[64,8,1024]{2,1,0:T(8,128)(2,1)}), bf16[64,8,1024]{2,1,0:T(8,128)(2,1)}, u32[]{:S(2)}, u32[]{:S(2)}) async-start(bf16[64,8,1024]{2,1,0:T(8,128)(2,1)} %copy.52), calls=%async_computation.2 | async-start | bytes 2097152 | tf_op jit(solution)/shard_map/all_to_all | solution.py:111
  416.2 33.5 %copy-start.1 = (bf16[1024,1024]{1,0:T(8,128)(2,1)S(1)}, bf16[1024,1024]{1,0:T(8,128)(2,1)}, u32[]{:S(2)}) copy-start(bf16[1024,1024]{1,0:T(8,128)(2,1)} %param.10) | copy-start | bytes 6291460
Sparse Core Ops, SparseCore 0:
  304.6 84.0 all-gather.1
